TPU v7x, 128 devices: a whole 4x4x4 slice. The times are simulated.
128 devices in a mesh: seq: 64 (over z, x, y_lo, core), chan: 2 (over y_hi).
Axes of the slice: x: 4, y: 4 (y_hi: 2, y_lo: 2; y = y_hi * 2 + y_lo), z: 4, core: 2. Of those that a mesh axis runs over, the one named last changes fastest.
Arguments:
- signal: bfloat16 [2, 32768, 128], P('chan', 'seq'), may hold values from -6 to 6
- cotangent: bfloat16 [2, 32768, 128], P('chan', 'seq'), may hold values from -6 to 6
- band_freq: int32 [16], replicated, may hold values from 1 to 8191
- w_embed: float32 [32, 64], replicated, may hold values from -2 to 2
- b_embed: float32 [64], replicated, may hold values from -3.140625 to 3.140625
- w_out: float32 [64, 128], P(None, 'chan'), may hold values from -0.75 to 0.75
- decay: float32 [128], P('chan'), may hold values from 0.25 to 16, as said below
Outputs:
- conv_out: bfloat16 [2, 32768, 128], P('chan', 'seq')
- d_signal: bfloat16 [2, 32768, 128], P('chan', 'seq')
- grad_embed: float32 [32, 64], replicated
- grad_bias: float32 [64], replicated
- grad_out: float32 [64, 128], P(None, 'chan')
Inputs may be any that keep to these rules, and one draw needn't show every extreme that they name: decay rates are positive.
All inputs are finite; a program needn't handle non-finite values.
Results may differ from a plain program's by a relative error of at most 0.007.
Values may be sent and summed in bfloat16 or wider, within the bound.
No kernel may reach another device: no remote copies, remote signals or barrier semaphores. Data moves between devices by JAX's collectives and lax.ppermute only.
A program may use at most 192 MiB of HBM per device.

v0:
```python
import math
import jax
import jax.numpy as jnp
from jax import lax
from jax.sharding import PartitionSpec as P

exact_mode = lax.Precision.HIGHEST


def mat_dot(lhs_mat, rhs_mat):
    return jnp.dot(lhs_mat, rhs_mat, preferred_element_type=jnp.float32, precision=exact_mode)


def band_phase(band_freq, places, seq_total):
    upper_part = places // 1024
    lower_part = places % 1024
    partial_turn = upper_part[:, None] * band_freq[None, :] % seq_total
    wrapped = (partial_turn * 1024 + lower_part[:, None] * band_freq[None, :]) % seq_total
    return wrapped.astype(jnp.float32) * (2.0 * math.pi / seq_total)


def filter_parts(places, band_freq, w_embed, b_embed, w_out, decay, seq_total):
    phases = band_phase(band_freq, places, seq_total)
    features = jnp.concatenate([jnp.cos(phases), jnp.sin(phases)], axis=1)
    preact = mat_dot(features, w_embed) + b_embed[None, :]
    hidden = jnp.sin(preact)
    fraction = places.astype(jnp.float32) / seq_total
    envelope = (
        jnp.exp(-decay[None, :] * fraction[:, None]) * jnp.sqrt((1.0 + decay) / seq_total)[None, :]
    )
    taps = mat_dot(hidden, w_out) * envelope
    return (features, preact, hidden, taps, envelope)


def angle_table(rows_idx, cols_idx, modulus):
    wrapped = rows_idx[:, None] * cols_idx[None, :] % modulus
    angles = wrapped.astype(jnp.float32) * (2.0 * math.pi / modulus)
    return (jnp.cos(angles), jnp.sin(angles))


def local(signal, cotangent, band_freq, w_embed, b_embed, w_out, decay):
    devices = lax.axis_size("seq")
    rank_seq = lax.axis_index("seq")
    seg_len = signal.shape[1] * 2
    channels = signal.shape[2] // 2
    block_w = seg_len // devices
    width = block_w * channels
    rows_all = 2 * devices
    pair = rows_all // devices
    seq_total = seg_len * devices
    fft_size = 2 * seq_total
    inv_scale = 1.0 / fft_size
    n_arr = 3
    dev_ids = jnp.arange(devices, dtype=jnp.int32)
    row_ids = jnp.arange(rows_all, dtype=jnp.int32)
    blk_ids = jnp.arange(block_w, dtype=jnp.int32)
    lane_blk = jnp.arange(width, dtype=jnp.int32) // channels
    b_lane = rank_seq * block_w + lane_blk
    src = jnp.stack([signal.reshape(devices, width), cotangent.reshape(devices, width)], axis=1)
    cols = lax.all_to_all(src, "seq", split_axis=0, concat_axis=0, tiled=True)
    places = (dev_ids[:, None] * seg_len + rank_seq * block_w + blk_ids[None, :]).reshape(-1)
    features, preact, hidden, taps, envelope = filter_parts(
        places, band_freq, w_embed, b_embed, w_out, decay, seq_total
    )
    stacked = jnp.concatenate(
        [cols.astype(jnp.float32), taps.reshape(devices, 1, width)], axis=1
    ).reshape(devices, n_arr * width)
    col_cos, col_sin = angle_table(row_ids, dev_ids, rows_all)
    y_re = mat_dot(col_cos, stacked).reshape(rows_all, n_arr, width)
    y_im = -mat_dot(col_sin, stacked).reshape(rows_all, n_arr, width)
    tw_cos, tw_sin = angle_table(row_ids, b_lane, fft_size)
    tw_cos = tw_cos[:, None, :]
    tw_sin = tw_sin[:, None, :]
    t_re = y_re * tw_cos + y_im * tw_sin
    t_im = y_im * tw_cos - y_re * tw_sin
    spec = jnp.stack([t_re, t_im], axis=1)
    spec = lax.all_to_all(spec, "seq", split_axis=0, concat_axis=0, tiled=True)
    q_cos, q_sin = angle_table(dev_ids, dev_ids, devices)
    stage_a = mat_dot(jnp.concatenate([q_cos, q_sin], axis=0), spec.reshape(devices, -1))
    stage_a = stage_a.reshape(2, devices, pair, 2, n_arr, width)
    a_re = stage_a[0, :, :, 0] + stage_a[1, :, :, 1]
    a_im = stage_a[0, :, :, 1] - stage_a[1, :, :, 0]
    mid_cos, mid_sin = angle_table(dev_ids, lane_blk, seg_len)
    mid_cos = mid_cos[:, None, None, :]
    mid_sin = mid_sin[:, None, None, :]
    b_re = (a_re * mid_cos + a_im * mid_sin).reshape(devices, pair, n_arr, block_w, channels)
    b_im = (a_im * mid_cos - a_re * mid_sin).reshape(devices, pair, n_arr, block_w, channels)
    m_cos, m_sin = angle_table(blk_ids, blk_ids, block_w)

    def blk_mix(table, vals):
        return jnp.einsum(
            "mb,qkzbc->qkzmc", table, vals, preferred_element_type=jnp.float32, precision=exact_mode
        )

    s_re = blk_mix(m_cos, b_re) + blk_mix(m_sin, b_im)
    s_im = blk_mix(m_cos, b_im) - blk_mix(m_sin, b_re)
    sig_r, cot_r, tap_r = (s_re[:, :, 0], s_re[:, :, 1], s_re[:, :, 2])
    sig_i, cot_i, tap_i = (s_im[:, :, 0], s_im[:, :, 1], s_im[:, :, 2])
    prod_r = jnp.stack(
        [
            sig_r * tap_r - sig_i * tap_i,
            cot_r * tap_r + cot_i * tap_i,
            cot_r * sig_r + cot_i * sig_i,
        ],
        axis=2,
    )
    prod_i = jnp.stack(
        [
            sig_r * tap_i + sig_i * tap_r,
            cot_i * tap_r - cot_r * tap_i,
            cot_i * sig_r - cot_r * sig_i,
        ],
        axis=2,
    )
    u_re = blk_mix(m_cos, prod_r) - blk_mix(m_sin, prod_i)
    u_im = blk_mix(m_cos, prod_i) + blk_mix(m_sin, prod_r)
    u_re = u_re.reshape(devices, pair, n_arr, width)
    u_im = u_im.reshape(devices, pair, n_arr, width)
    v_re = u_re * mid_cos - u_im * mid_sin
    v_im = u_im * mid_cos + u_re * mid_sin
    v_all = jnp.stack([v_re, v_im]).reshape(2 * devices, -1)
    inv_mat = jnp.concatenate(
        [jnp.concatenate([q_cos, -q_sin], axis=1), jnp.concatenate([q_sin, q_cos], axis=1)], axis=0
    )
    w_all = mat_dot(inv_mat, v_all).reshape(2, devices, pair, n_arr, width)
    b_rows = dev_ids[:, None] * block_w + lane_blk[None, :]
    k1_own = rank_seq * pair + jnp.arange(pair, dtype=jnp.int32)
    ex_ang = b_rows[:, None, :] * k1_own[None, :, None] % fft_size
    ex_ang = ex_ang.astype(jnp.float32) * (2.0 * math.pi / fft_size)
    ex_cos = jnp.cos(ex_ang)[:, :, None, :]
    ex_sin = jnp.sin(ex_ang)[:, :, None, :]
    x_re = w_all[0] * ex_cos - w_all[1] * ex_sin
    x_im = w_all[0] * ex_sin + w_all[1] * ex_cos
    back = jnp.stack([x_re, x_im], axis=1)
    back = lax.all_to_all(back, "seq", split_axis=0, concat_axis=0, tiled=True)
    back = back.reshape(devices, 2, pair, n_arr * width)
    back = jnp.transpose(back, (1, 0, 2, 3)).reshape(2 * rows_all, n_arr * width)
    out_mat = jnp.concatenate([col_cos.T, -col_sin.T], axis=1)
    res = (mat_dot(out_mat, back) * inv_scale).reshape(devices, n_arr, width)
    rows_out = lax.all_to_all(
        res[:, 0:2].astype(jnp.bfloat16), "seq", split_axis=0, concat_axis=0, tiled=True
    )
    conv_out = rows_out[:, 0].reshape(1, seg_len // 2, 2 * channels)
    d_signal = rows_out[:, 1].reshape(1, seg_len // 2, 2 * channels)
    d_taps = res[:, 2].reshape(devices * block_w, channels)
    d_raw = d_taps * envelope
    d_preact = mat_dot(d_raw, w_out.T) * jnp.cos(preact)
    out_part = mat_dot(hidden.T, d_raw)
    embed_part = mat_dot(features.T, d_preact)
    bias_part = jnp.sum(d_preact, axis=0)
    out_sum = lax.psum(out_part, "seq")
    embed_all, bias_all = lax.psum((embed_part, bias_part), ("seq", "chan"))
    norm_scale = 1.0 / math.sqrt(seq_total)
    return (conv_out, d_signal, embed_all * norm_scale, bias_all * norm_scale, out_sum * norm_scale)


def solution(mesh):
    return jax.shard_map(
        local,
        mesh=mesh,
        in_specs=(
            P("chan", "seq", None),
            P("chan", "seq", None),
            P(),
            P(),
            P(),
            P(None, "chan"),
            P("chan"),
        ),
        out_specs=(P("chan", "seq", None), P("chan", "seq", None), P(), P(), P(None, "chan")),
        check_vma=False,
    )
```

profile of v0, /device:TPU:0, one launch (start us, length us, event | category | flops | bytes accessed | tf_op | source)
XLA Modules:
  0.0 615.8 jit_solution(7838954913175535610)
XLA Ops:
  4.4 9.9 %all-to-all-start = ((bf16[64,2,1024]{2,1,0:T(2,128)(2,1)}), bf16[64,2,1024]{2,1,0:T(2,128)(2,1)S(1)}, u32[]{:S(2)}, u32[]{:S(2)}) async-start(bf16[64,2,1024]{2,1,0:T(2,128)(2,1)} %pad_maximum_fusion.14), calls=%async_computation | async-start | bytes 524288 | tf_op jit(solution)/shard_map/all_to_all | solution.py:60
  29.3 4.1 copy.76
  33.4 6.9 %all-to-all-start.1 = ((f32[128,2,3,1024]{3,1,2,0:T(2,128)}), f32[128,2,3,1024]{3,1,2,0:T(2,128)S(1)}, u32[]{:S(2)}, u32[]{:S(2)}) async-start(f32[128,2,3,1024]{3,1,2,0:T(2,128)} %copy.76), calls=%async_computation.1 | async-start | bytes 6291456 | tf_op jit(solution)/shard_map/all_to_all | solution.py:77
  47.2 9.5 %fusion.38 = (f32[64,2,1024]{2,1,0:T(2,128)}, f32[64,2,1024]{2,1,0:T(2,128)}) fusion(s32[2]{0:T(128)S(1)} %iota_add_fusion.1, s32[64,1024]{1,0:T(8,128)S(1)} %broadcast_add_fusion), kind=kLoop, calls=%fused_computation.88 | loop fusion | flops 1835008 | bytes 1310728 | tf_op jit(solution)/shard_map/cos | solution.py:130
  56.8 23.2 %all-to-all-done.1 = f32[128,2,3,1024]{3,1,2,0:T(2,128)S(1)} async-done(((f32[128,2,3,1024]{3,1,2,0:T(2,128)}), f32[128,2,3,1024]{3,1,2,0:T(2,128)S(1)}, u32[]{:S(2)}, u32[]{:S(2)}) %all-to-all-start.1) | async-done | bytes 3145760 | tf_op jit(solution)/shard_map/all_to_all | solution.py:77
  80.0 3.7 copy.77
  83.7 4.3 reshape.397
  88.0 3.7 dot_general.72
  91.8 9.4 %fusion = f32[2,64,2,2,3,1024]{5,1,4,3,2,0:T(8,128)S(1)} fusion(f32[2,64,64,1,1,1]{2,1,5,4,3,0:T(8,128)} %bitcast.98, f32[2,2,3,1024,64]{3,2,1,0,4:T(4,128)} %dot_general.72), kind=kOutput, calls=%fused_computation.6 | convolution fusion | flops 1207959552 | bytes 9469952 | tf_op jit(solution)/shard_map/dot_general | solution.py:11
  106.4 3.6 sub.92
  110.0 5.5 fusion.51
  122.1 3.5 subtract_bitcast_fusion.1
  132.9 4.7 subtract_bitcast_fusion
  137.6 4.9 reshape.411
  142.5 6.4 %add_bitcast_fusion = f32[64,2,3,16,64]{4,3,2,1,0:T(8,128)} fusion(f32[64,2,3,64,16]{3,4,2,1,0:T(8,128)S(1)} %fusion.3, f32[64,2,1,16,64]{4,3,2,1,0:T(8,128)} %copy-done.5, f32[64,2,1,16,64]{4,3,2,1,0:T(8,128)} %copy-done.6, f32[64,2,1,16,64]{4,3,2,1,0:T(8,128)} %copy-done.4), kind=kOutput, calls=%fused_computation.9 | convolution fusion | flops 76680704 | bytes 4718592 | tf_op jit(solution)/shard_map/mb,qkzbc->qkzmc/dot_general | solution.py:91
  148.9 4.6 reshape.412
  153.6 3.3 multiply_subtract_fusion.2
  157.1 4.1 copy.85
  161.2 5.0 reshape.400
  166.2 3.8 fusion.63
  174.9 3.9 squeeze.5
  182.9 4.7 copy.86
  187.5 6.6 %all-to-all-start.2 = ((f32[64,2,2,3,1024]{4,2,3,1,0:T(2,128)}), f32[64,2,2,3,1024]{4,2,3,1,0:T(2,128)S(1)}, u32[]{:S(2)}, u32[]{:S(2)}) async-start(f32[64,2,2,3,1024]{4,2,3,1,0:T(2,128)} %copy.86), calls=%async_computation.2 | async-start | bytes 6291456 | tf_op jit(solution)/shard_map/all_to_all | solution.py:135
  194.9 38.9 %all-to-all-done.2 = f32[64,2,2,3,1024]{4,2,3,1,0:T(2,128)S(1)} async-done(((f32[64,2,2,3,1024]{4,2,3,1,0:T(2,128)}), f32[64,2,2,3,1024]{4,2,3,1,0:T(2,128)S(1)}, u32[]{:S(2)}, u32[]{:S(2)}) %all-to-all-start.2) | async-done | bytes 3145760 | tf_op jit(solution)/shard_map/all_to_all | solution.py:135
  233.8 3.6 copy.87
  237.4 5.0 reshape.401
  242.3 4.1 copy.88
  246.4 3.9 reshape.402
  250.3 3.7 convolution_multiply_fusion
  259.9 64.6 %all-reduce = (f32[32,64]{1,0:T(8,128)S(1)}, f32[64]{0:T(128)S(1)}) all-reduce(f32[32,64]{1,0:T(8,128)S(1)} %fusion.53, f32[64]{0:T(128)S(1)} %get-tuple-element.41), channel_id=1, replica_groups=mesh['seq'=64,'chan'=2] {'seq','chan'}, use_global_device_ids=true, to_apply=%region_0.1 | all-reduce | flops 2112 | bytes 16896 | tf_op jit(solution)/shard_map/psum | solution.py:152
  325.1 5.9 all-to-all-start.3
  331.5 280.7 %psum.23 = f32[64,64]{1,0:T(8,128)S(1)} all-reduce(f32[64,64]{1,0:T(8,128)S(1)} %fusion.40), channel_id=1, replica_groups=mesh['seq'=64,'chan'=2] {'seq'}, use_global_device_ids=true, to_apply=%region_3.4 | all-reduce | flops 4096 | bytes 32768 | tf_op jit(solution)/shard_map/psum | solution.py:151
  (93 shorter events, 64.6 us)
Async XLA Ops:
  0.6 18.3 %copy-start = (f32[64,64]{1,0:T(8,128)S(1)}, f32[64,64]{1,0:T(8,128)}, u32[]{:S(2)}) copy-start(f32[64,64]{1,0:T(8,128)} %param.12) | copy-start | bytes 49156
  4.4 19.8 %all-to-all-start = ((bf16[64,2,1024]{2,1,0:T(2,128)(2,1)}), bf16[64,2,1024]{2,1,0:T(2,128)(2,1)S(1)}, u32[]{:S(2)}, u32[]{:S(2)}) async-start(bf16[64,2,1024]{2,1,0:T(2,128)(2,1)} %pad_maximum_fusion.14), calls=%async_computation | async-start | bytes 524288 | tf_op jit(solution)/shard_map/all_to_all | solution.py:60
  16.2 2.7 copy-start.13
  33.4 46.6 %all-to-all-start.1 = ((f32[128,2,3,1024]{3,1,2,0:T(2,128)}), f32[128,2,3,1024]{3,1,2,0:T(2,128)S(1)}, u32[]{:S(2)}, u32[]{:S(2)}) async-start(f32[128,2,3,1024]{3,1,2,0:T(2,128)} %copy.76), calls=%async_computation.1 | async-start | bytes 6291456 | tf_op jit(solution)/shard_map/all_to_all | solution.py:77
  41.2 0.6 copy-start.15
  109.9 5.5 copy-start.1
  110.0 5.5 copy-start.2
  110.0 5.5 copy-start.3
  126.2 6.8 %copy-start.6 = (f32[64,2,1,16,64]{4,3,2,1,0:T(8,128)}, f32[64,2,1,16,64]{4,3,2,1,0:T(8,128)S(1)}, u32[]{:S(2)}) copy-start(f32[64,2,1,16,64]{4,3,2,1,0:T(8,128)S(1)} %get-tuple-element.13) | copy-start | bytes 1572868
  126.9 6.0 copy-start.4
  126.9 6.0 copy-start.5
  148.9 4.6 copy-start.7
  148.9 4.6 copy-start.10
  148.9 4.6 copy-start.11
  171.9 7.0 %copy-start.8 = (f32[64,2,1024]{2,1,0:T(2,128)S(1)}, f32[64,2,1024]{2,1,0:T(2,128)}, u32[]{:S(2)}) copy-start(f32[64,2,1024]{2,1,0:T(2,128)} %get-tuple-element.25) | copy-start | bytes 1572868
  171.9 7.0 %copy-start.9 = (f32[64,2,1024]{2,1,0:T(2,128)S(1)}, f32[64,2,1024]{2,1,0:T(2,128)}, u32[]{:S(2)}) copy-start(f32[64,2,1024]{2,1,0:T(2,128)} %get-tuple-element.26) | copy-start | bytes 1572868
  187.5 46.3 %all-to-all-start.2 = ((f32[64,2,2,3,1024]{4,2,3,1,0:T(2,128)}), f32[64,2,2,3,1024]{4,2,3,1,0:T(2,128)S(1)}, u32[]{:S(2)}, u32[]{:S(2)}) async-start(f32[64,2,2,3,1024]{4,2,3,1,0:T(2,128)} %copy.86), calls=%async_computation.2 | async-start | bytes 6291456 | tf_op jit(solution)/shard_map/all_to_all | solution.py:135
  254.0 4.2 copy-start.12
  254.0 5.6 copy-start.14
  325.1 287.8 %all-to-all-start.3 = ((bf16[64,2,1024]{2,1,0:T(2,128)(2,1)}), bf16[64,2,1024]{2,1,0:T(2,128)(2,1)S(1)}, u32[]{:S(2)}, u32[]{:S(2)}) async-start(bf16[64,2,1024]{2,1,0:T(2,128)(2,1)} %slice.117), calls=%async_computation.3 | async-start | bytes 524288 | tf_op jit(solution)/shard_map/all_to_all | solution.py:140
where the time goes:
time: 627 us; the launch traced here: 616 us
  blocking collectives  345 us (55%)
  local copies, waits for them, and re-layouts  80.4 us (13%)
  waiting for transfers between devices  64.5 us (10%)
  matrix products  58.9 us (9%)
  other arithmetic  35.8 us (6%)
  starting transfers between devices  29.3 us (5%)
    psum x1, blocking collectives, local(): out_sum = lax.psum(out_part, 'seq')  281 us
    psum x1, blocking collectives, local(): embed_all, bias_all = lax.psum((embed_part, bias_part), ('seq', 'chan'))  64.6 us
    all_to_all x1, waiting for transfers between devices, local(): back = lax.all_to_all(back, 'seq', split_axis=0, concat_axis=0, tiled=True)  38.9 us
    dot_general x8, matrix products, blk_mix(): jnp.einsum('mb,qkzbc->qkzmc', table, vals, preferred_element_type=jnp.flo...  32.6 us
    dot_general x10, matrix products, mat_dot(): jnp.dot(lhs_mat, rhs_mat, preferred_element_type=jnp.float32, precision=e...  26.2 us
    all_to_all x1, waiting for transfers between devices, local(): spec = lax.all_to_all(spec, 'seq', split_axis=0, concat_axis=0, tiled=True)  23.2 us
  transfers between devices with their start and end apart: 4, of which 3 were waited for; matrix products, arithmetic and copies ran while one was open for 4% of the time, Pallas kernels for 0%

commit v1 on v0

--- a/solution.py
+++ b/solution.py
@@ -148,7 +148,7 @@
     out_part = mat_dot(hidden.T, d_raw)
     embed_part = mat_dot(features.T, d_preact)
     bias_part = jnp.sum(d_preact, axis=0)
-    out_sum = lax.psum(out_part, "seq")
+    out_sum = jnp.sum(lax.all_gather(out_part, "seq"), axis=0)
     embed_all, bias_all = lax.psum((embed_part, bias_part), ("seq", "chan"))
     norm_scale = 1.0 / math.sqrt(seq_total)
     return (conv_out, d_signal, embed_all * norm_scale, bias_all * norm_scale, out_sum * norm_scale)

time: 627 us -> 383 us (0.61)
  blocking collectives: 345 us -> 67.7 us
  waiting for transfers between devices: 64.5 us -> 87.6 us
  between operations: 1.63 us -> 14.8 us
    psum x1 -> x0, blocking collectives: 281 us -> none  [local(): out_sum = lax.psum(out_part, 'seq')]
    all_gather x0 -> x1, waiting for transfers between devices: none -> 23.1 us  [local(): out_sum = jnp.sum(lax.all_gather(out_part, 'seq'), axis=0)]
  transfers between devices with their start and end apart: 4 -> 5, of which waited for: 3 -> 4; matrix products, arithmetic and copies ran while one was open for 4% -> 8% of each run, Pallas kernels for 0% -> 0%
where the time goes in v1:
time: 383 us; the launch traced here: 378 us
  waiting for transfers between devices  87.6 us (23%)
  local copies, waits for them, and re-layouts  80.6 us (21%)
  blocking collectives  67.7 us (18%)
  matrix products  59.5 us (16%)
  other arithmetic  37.6 us (10%)
  starting transfers between devices  29.9 us (8%)
  between operations  14.8 us (4%)
    psum x1, blocking collectives, local(): embed_all, bias_all = lax.psum((embed_part, bias_part), ('seq', 'chan'))  67.7 us
    all_to_all x1, waiting for transfers between devices, local(): back = lax.all_to_all(back, 'seq', split_axis=0, concat_axis=0, tiled=True)  38.9 us
    dot_general x8, matrix products, blk_mix(): jnp.einsum('mb,qkzbc->qkzmc', table, vals, preferred_element_type=jnp.flo...  32.7 us
    dot_general x10, matrix products, mat_dot(): jnp.dot(lhs_mat, rhs_mat, preferred_element_type=jnp.float32, precision=e...  26.8 us
    all_to_all x1, waiting for transfers between devices, local(): spec = lax.all_to_all(spec, 'seq', split_axis=0, concat_axis=0, tiled=True)  23.3 us
    all_gather x1, waiting for transfers between devices, local(): out_sum = jnp.sum(lax.all_gather(out_part, 'seq'), axis=0)  23.1 us
    all_to_all x1, starting transfers between devices, local(): cols = lax.all_to_all(src, 'seq', split_axis=0, concat_axis=0, tiled=True)  10.1 us
    cos x1, other arithmetic, local(): ex_cos = jnp.cos(ex_ang)[:, :, None, :]  9.49 us
  transfers between devices with their start and end apart: 5, of which 4 were waited for; matrix products, arithmetic and copies ran while one was open for 8% of the time, Pallas kernels for 0%

profile of v1, /device:TPU:0, one launch (start us, length us, event | category | flops | bytes accessed | tf_op | source)
XLA Modules:
  0.0 377.8 jit_solution(7627434886997407737)
XLA Ops:
  11.0 10.1 %all-to-all-start = ((bf16[64,2,1024]{2,1,0:T(2,128)(2,1)}), bf16[64,2,1024]{2,1,0:T(2,128)(2,1)S(1)}, u32[]{:S(2)}, u32[]{:S(2)}) async-start(bf16[64,2,1024]{2,1,0:T(2,128)(2,1)} %pad_maximum_fusion.14), calls=%async_computation | async-start | bytes 524288 | tf_op jit(solution)/shard_map/all_to_all | solution.py:60
  36.0 4.1 %copy.76 = f32[128,2,3,1024]{3,1,2,0:T(2,128)} copy(f32[128,2,3,1024]{3,0,2,1:T(8,128)S(1)} %pad_maximum_fusion.1) | data formatting | bytes 6291456 | tf_op jit(solution)/shard_map/stack | solution.py:76
  40.1 7.0 %all-to-all-start.1 = ((f32[128,2,3,1024]{3,1,2,0:T(2,128)}), f32[128,2,3,1024]{3,1,2,0:T(2,128)S(1)}, u32[]{:S(2)}, u32[]{:S(2)}) async-start(f32[128,2,3,1024]{3,1,2,0:T(2,128)} %copy.76), calls=%async_computation.1 | async-start | bytes 6291456 | tf_op jit(solution)/shard_map/all_to_all | solution.py:77
  54.1 9.5 %fusion.38 = (f32[64,2,1024]{2,1,0:T(2,128)}, f32[64,2,1024]{2,1,0:T(2,128)}) fusion(s32[2]{0:T(128)S(1)} %iota_add_fusion.1, s32[64,1024]{1,0:T(8,128)S(1)} %broadcast_add_fusion), kind=kLoop, calls=%fused_computation.88 | loop fusion | flops 1835008 | bytes 1310728 | tf_op jit(solution)/shard_map/cos | solution.py:130
  63.6 23.3 %all-to-all-done.1 = f32[128,2,3,1024]{3,1,2,0:T(2,128)S(1)} async-done(((f32[128,2,3,1024]{3,1,2,0:T(2,128)}), f32[128,2,3,1024]{3,1,2,0:T(2,128)S(1)}, u32[]{:S(2)}, u32[]{:S(2)}) %all-to-all-start.1) | async-done | bytes 3145760 | tf_op jit(solution)/shard_map/all_to_all | solution.py:77
  86.9 3.7 copy.77
  90.6 4.3 %reshape.397 = f32[64,12288]{1,0:T(8,128)S(1)} reshape(f32[128,2,3,1024]{3,2,1,0:T(4,128)} %copy.77) | data formatting | bytes 6291456 | tf_op jit(solution)/shard_map/reshape | solution.py:79
  94.9 3.7 dot_general.72
  98.6 9.4 %fusion = f32[2,64,2,2,3,1024]{5,1,4,3,2,0:T(8,128)S(1)} fusion(f32[2,64,64,1,1,1]{2,1,5,4,3,0:T(8,128)} %bitcast.100, f32[2,2,3,1024,64]{3,2,1,0,4:T(4,128)} %dot_general.72), kind=kOutput, calls=%fused_computation.6 | convolution fusion | flops 1207959552 | bytes 9469952 | tf_op jit(solution)/shard_map/dot_general | solution.py:11
  113.2 3.6 sub.92
  116.8 5.5 %fusion.51 = f32[64,2,3,64,16]{3,4,2,1,0:T(8,128)S(1)} fusion(f32[64,2,3,16,64]{4,3,0,2,1:T(8,128)} %sub.92, f32[64,2,3,16,64]{4,3,0,2,1:T(8,128)S(1)} %add.317, f32[64,16,64]{2,1,0:T(8,128)} %get-tuple-element.30, f32[64,16,64]{2,1,0:T(8,128)} %get-tuple-element.29), kind=kOutput, calls=%fused_computation.104 | convolution fusion | flops 76680704 | bytes 5242880 | tf_op jit(solution)/shard_map/mb,qkzbc->qkzmc/dot_general | solution.py:91
  129.0 3.5 subtract_bitcast_fusion.1
  139.8 4.7 %subtract_bitcast_fusion = f32[64,2,3,16,64]{4,3,2,1,0:T(8,128)} fusion(f32[64,2,3,64,16]{3,4,2,1,0:T(8,128)S(1)} %fusion.4, f32[64,2,1,16,64]{4,3,2,1,0:T(8,128)S(1)} %get-tuple-element.10, f32[64,2,1,16,64]{4,3,2,1,0:T(8,128)S(1)} %get-tuple-element.13, f32[64,2,1,16,64]{4,3,2,1,0:T(8,128)S(1)} %get-tuple-element.9), kind=kOutput, calls=%fused_computation.10 | convolution fusion | flops 76680704 | bytes 4718592 | tf_op jit(solution)/shard_map/mb,qkzbc->qkzmc/dot_general | solution.py:91
  144.5 4.9 %reshape.412 = f32[1,64,2,3,1024]{4,3,2,1,0:T(4,128)} reshape(f32[64,2,3,16,64]{4,3,2,1,0:T(8,128)} %subtract_bitcast_fusion) | data formatting | bytes 3145728 | tf_op jit(solution)/shard_map/reshape | solution.py:117
  149.4 6.4 %add_bitcast_fusion = f32[64,2,3,16,64]{4,3,2,1,0:T(8,128)} fusion(f32[64,2,3,64,16]{3,4,2,1,0:T(8,128)S(1)} %fusion.3, f32[64,2,1,16,64]{4,3,2,1,0:T(8,128)} %copy-done.5, f32[64,2,1,16,64]{4,3,2,1,0:T(8,128)} %copy-done.6, f32[64,2,1,16,64]{4,3,2,1,0:T(8,128)} %copy-done.4), kind=kOutput, calls=%fused_computation.9 | convolution fusion | flops 76680704 | bytes 4718592 | tf_op jit(solution)/shard_map/mb,qkzbc->qkzmc/dot_general | solution.py:91
  155.8 4.6 %reshape.413 = f32[1,64,2,3,1024]{4,3,2,1,0:T(4,128)} reshape(f32[64,2,3,16,64]{4,3,2,1,0:T(8,128)} %add_bitcast_fusion) | data formatting | bytes 3145728 | tf_op jit(solution)/shard_map/reshape | solution.py:118
  160.5 3.3 multiply_subtract_fusion.2
  164.0 4.1 %copy.85 = f32[2,64,2,3,1024]{4,3,2,1,0:T(4,128)} copy(f32[2,64,2,3,1024]{4,1,3,2,0:T(8,128)S(1)} %pad_maximum_fusion.4) | data formatting | bytes 6291456 | tf_op jit(solution)/shard_map/stack | solution.py:121
  168.1 5.0 %reshape.400 = f32[128,6144]{1,0:T(8,128)S(1)} reshape(f32[2,64,2,3,1024]{4,3,2,1,0:T(4,128)} %copy.85) | data formatting | bytes 6291456 | tf_op jit(solution)/shard_map/reshape | solution.py:121
  173.1 3.8 %fusion.63 = f32[128,6144]{1,0:T(8,128)S(1)} fusion(f32[128,6144]{1,0:T(8,128)S(1)} %reshape.400, f32[64,64]{1,0:T(8,128)} %copy-done.15, f32[64,64]{1,0:T(8,128)S(1)} %get-tuple-element.43, f32[64,64]{1,0:T(8,128)} %fusion.100), kind=kOutput, calls=%fused_computation.121 | convolution fusion | flops 1208008704 | bytes 6340608 | tf_op jit(solution)/shard_map/dot_general | solution.py:11
  181.8 3.9 %squeeze.5 = f32[64,1,2,3,1024]{4,3,2,0,1:T(4,128)} reshape(f32[64,6144]{1,0:T(8,128)} %get-tuple-element.24) | data formatting | bytes 3145728 | tf_op jit(solution)/shard_map/squeeze | solution.py:132
  189.8 4.7 %copy.86 = f32[64,2,2,3,1024]{4,2,3,1,0:T(2,128)} copy(f32[64,2,2,3,1024]{4,3,2,0,1:T(4,128)S(1)} %pad_maximum_fusion) | data formatting | bytes 6291456 | tf_op jit(solution)/shard_map/stack | solution.py:134
  194.4 6.4 %all-to-all-start.2 = ((f32[64,2,2,3,1024]{4,2,3,1,0:T(2,128)}), f32[64,2,2,3,1024]{4,2,3,1,0:T(2,128)S(1)}, u32[]{:S(2)}, u32[]{:S(2)}) async-start(f32[64,2,2,3,1024]{4,2,3,1,0:T(2,128)} %copy.86), calls=%async_computation.2 | async-start | bytes 6291456 | tf_op jit(solution)/shard_map/all_to_all | solution.py:135
  201.6 38.9 %all-to-all-done.2 = f32[64,2,2,3,1024]{4,2,3,1,0:T(2,128)S(1)} async-done(((f32[64,2,2,3,1024]{4,2,3,1,0:T(2,128)}), f32[64,2,2,3,1024]{4,2,3,1,0:T(2,128)S(1)}, u32[]{:S(2)}, u32[]{:S(2)}) %all-to-all-start.2) | async-done | bytes 3145760 | tf_op jit(solution)/shard_map/all_to_all | solution.py:135
  240.6 3.6 copy.87
  244.2 5.2 %reshape.401 = f32[64,2,2,3072]{3,0,2,1:T(8,128)S(1)} reshape(f32[64,2,2,3,1024]{4,3,0,2,1:T(4,128)} %copy.87) | data formatting | bytes 6291456 | tf_op jit(solution)/shard_map/reshape | solution.py:136
  249.3 4.1 %copy.88 = f32[2,64,2,3072]{3,2,1,0:T(2,128)} copy(f32[2,64,2,3072]{3,1,2,0:T(8,128)S(1)} %bitcast.96) | data formatting | bytes 6291456 | tf_op jit(solution)/shard_map/transpose | solution.py:137
  253.4 3.9 %reshape.402 = f32[256,3072]{1,0:T(8,128)S(1)} reshape(f32[2,64,2,3072]{3,2,1,0:T(2,128)} %copy.88) | data formatting | bytes 6291456 | tf_op jit(solution)/shard_map/reshape | solution.py:137
  257.3 3.7 convolution_multiply_fusion
  265.8 6.4 %all-to-all-start.3 = ((bf16[64,2,1024]{2,1,0:T(2,128)(2,1)}), bf16[64,2,1024]{2,1,0:T(2,128)(2,1)S(1)}, u32[]{:S(2)}, u32[]{:S(2)}) async-start(bf16[64,2,1024]{2,1,0:T(2,128)(2,1)} %slice.117), calls=%async_computation.3 | async-start | bytes 524288 | tf_op jit(solution)/shard_map/all_to_all | solution.py:140
  273.9 67.7 %all-reduce = (f32[32,64]{1,0:T(8,128)S(1)}, f32[64]{0:T(128)S(1)}) all-reduce(f32[32,64]{1,0:T(8,128)S(1)} %fusion.53, f32[64]{0:T(128)S(1)} %get-tuple-element.41), channel_id=1, replica_groups=mesh['seq'=64,'chan'=2] {'seq','chan'}, use_global_device_ids=true, to_apply=%region_0.1 | all-reduce | flops 2112 | bytes 16896 | tf_op jit(solution)/shard_map/psum | solution.py:152
  345.2 23.1 %all-gather.3.cloned.1.call-done = f32[4096,64]{1,0:T(8,128)} async-done(((f32[64,64]{1,0:T(8,128)}), f32[4096,64]{1,0:T(8,128)}) %all-gather.3.cloned.1.call-update) | async-done | bytes 1048592 | tf_op jit(solution)/shard_map/all_gather | solution.py:151
  (96 shorter events, 67.1 us)
Async XLA Ops:
  7.2 18.4 %copy-start = (f32[64,64]{1,0:T(8,128)S(1)}, f32[64,64]{1,0:T(8,128)}, u32[]{:S(2)}) copy-start(f32[64,64]{1,0:T(8,128)} %param.12) | copy-start | bytes 49156
  11.0 20.0 %all-to-all-start = ((bf16[64,2,1024]{2,1,0:T(2,128)(2,1)}), bf16[64,2,1024]{2,1,0:T(2,128)(2,1)S(1)}, u32[]{:S(2)}, u32[]{:S(2)}) async-start(bf16[64,2,1024]{2,1,0:T(2,128)(2,1)} %pad_maximum_fusion.14), calls=%async_computation | async-start | bytes 524288 | tf_op jit(solution)/shard_map/all_to_all | solution.py:60
  22.9 2.7 copy-start.13
  40.1 46.8 %all-to-all-start.1 = ((f32[128,2,3,1024]{3,1,2,0:T(2,128)}), f32[128,2,3,1024]{3,1,2,0:T(2,128)S(1)}, u32[]{:S(2)}, u32[]{:S(2)}) async-start(f32[128,2,3,1024]{3,1,2,0:T(2,128)} %copy.76), calls=%async_computation.1 | async-start | bytes 6291456 | tf_op jit(solution)/shard_map/all_to_all | solution.py:77
  48.1 0.6 copy-start.15
  116.8 5.5 %copy-start.1 = (f32[64,2,3,16,64]{4,3,0,2,1:T(8,128)S(1)}, f32[64,2,3,16,64]{4,3,0,2,1:T(8,128)}, u32[]{:S(2)}) copy-start(f32[64,2,3,16,64]{4,3,0,2,1:T(8,128)} %sub.92) | copy-start | bytes 4718596
  116.8 5.5 %copy-start.2 = (f32[64,16,64]{2,1,0:T(8,128)S(1)}, f32[64,16,64]{2,1,0:T(8,128)}, u32[]{:S(2)}) copy-start(f32[64,16,64]{2,1,0:T(8,128)} %get-tuple-element.29) | copy-start | bytes 786436
  116.8 5.5 %copy-start.3 = (f32[64,16,64]{2,1,0:T(8,128)S(1)}, f32[64,16,64]{2,1,0:T(8,128)}, u32[]{:S(2)}) copy-start(f32[64,16,64]{2,1,0:T(8,128)} %get-tuple-element.30) | copy-start | bytes 786436
  133.0 6.8 %copy-start.6 = (f32[64,2,1,16,64]{4,3,2,1,0:T(8,128)}, f32[64,2,1,16,64]{4,3,2,1,0:T(8,128)S(1)}, u32[]{:S(2)}) copy-start(f32[64,2,1,16,64]{4,3,2,1,0:T(8,128)S(1)} %get-tuple-element.13) | copy-start | bytes 1572868
  133.8 6.0 %copy-start.4 = (f32[64,2,1,16,64]{4,3,2,1,0:T(8,128)}, f32[64,2,1,16,64]{4,3,2,1,0:T(8,128)S(1)}, u32[]{:S(2)}) copy-start(f32[64,2,1,16,64]{4,3,2,1,0:T(8,128)S(1)} %get-tuple-element.9) | copy-start | bytes 1572868
  133.8 6.0 %copy-start.5 = (f32[64,2,1,16,64]{4,3,2,1,0:T(8,128)}, f32[64,2,1,16,64]{4,3,2,1,0:T(8,128)S(1)}, u32[]{:S(2)}) copy-start(f32[64,2,1,16,64]{4,3,2,1,0:T(8,128)S(1)} %get-tuple-element.10) | copy-start | bytes 1572868
  155.8 4.6 %copy-start.7 = (f32[1,64,2,3,1024]{4,3,2,1,0:T(4,128)S(1)}, f32[1,64,2,3,1024]{4,3,2,1,0:T(4,128)}, u32[]{:S(2)}) copy-start(f32[1,64,2,3,1024]{4,3,2,1,0:T(4,128)} %reshape.412) | copy-start | bytes 4718596
  155.8 4.6 %copy-start.10 = (f32[64,1024]{1,0:T(8,128)S(1)}, f32[64,1024]{1,0:T(8,128)}, u32[]{:S(2)}) copy-start(f32[64,1024]{1,0:T(8,128)} %get-tuple-element.31) | copy-start | bytes 786436
  155.8 4.6 %copy-start.11 = (f32[64,1024]{1,0:T(8,128)S(1)}, f32[64,1024]{1,0:T(8,128)}, u32[]{:S(2)}) copy-start(f32[64,1024]{1,0:T(8,128)} %get-tuple-element.32) | copy-start | bytes 786436
  178.8 7.0 %copy-start.8 = (f32[64,2,1024]{2,1,0:T(2,128)S(1)}, f32[64,2,1024]{2,1,0:T(2,128)}, u32[]{:S(2)}) copy-start(f32[64,2,1024]{2,1,0:T(2,128)} %get-tuple-element.25) | copy-start | bytes 1572868
  178.8 7.0 %copy-start.9 = (f32[64,2,1024]{2,1,0:T(2,128)S(1)}, f32[64,2,1024]{2,1,0:T(2,128)}, u32[]{:S(2)}) copy-start(f32[64,2,1024]{2,1,0:T(2,128)} %get-tuple-element.26) | copy-start | bytes 1572868
  194.4 46.2 %all-to-all-start.2 = ((f32[64,2,2,3,1024]{4,2,3,1,0:T(2,128)}), f32[64,2,2,3,1024]{4,2,3,1,0:T(2,128)S(1)}, u32[]{:S(2)}, u32[]{:S(2)}) async-start(f32[64,2,2,3,1024]{4,2,3,1,0:T(2,128)} %copy.86), calls=%async_computation.2 | async-start | bytes 6291456 | tf_op jit(solution)/shard_map/all_to_all | solution.py:135
  200.8 167.5 %all-gather.3.cloned.1.call-start = ((), (), s32[]{:S(2)}) async-start(), calls=%async_computation.4 | async-start | bytes 2129920 | tf_op jit(solution)/shard_map/all_gather | solution.py:151
  260.9 11.3 %copy-start.12 = (f32[1024,64]{0,1:T(8,128)S(1)}, f32[1024,64]{0,1:T(8,128)}, u32[]{:S(2)}) copy-start(f32[1024,64]{0,1:T(8,128)} %get-tuple-element.40) | copy-start | bytes 786436
  260.9 12.6 %copy-start.14 = (f32[1024,16]{0,1:T(8,128)S(1)}, f32[1024,16]{0,1:T(8,128)}, u32[]{:S(2)}) copy-start(f32[1024,16]{0,1:T(8,128)} %copy-done.13) | copy-start | bytes 196612
  265.8 76.9 %all-to-all-start.3 = ((bf16[64,2,1024]{2,1,0:T(2,128)(2,1)}), bf16[64,2,1024]{2,1,0:T(2,128)(2,1)S(1)}, u32[]{:S(2)}, u32[]{:S(2)}) async-start(bf16[64,2,1024]{2,1,0:T(2,128)(2,1)} %slice.117), calls=%async_computation.3 | async-start | bytes 524288 | tf_op jit(solution)/shard_map/all_to_all | solution.py:140
Sparse Core Ops, SparseCore 0:
  265.0 103.2 all-gather.2
